TPU v7x, 512 devices: a whole 4x4x16 slice. The times are simulated.
512 devices in a mesh: dp: 32 (over y, x, core), wide: 16 (over z).
Axes of the slice: x: 4, y: 4, z: 16, core: 2. Of those that a mesh axis runs over, the one named last changes fastest.
Arguments:
- trunk_out: bfloat16 [16384, 1024], P('dp'), may hold values from -6 to 6
- projection: bfloat16 [1024, 4096], P(None, 'wide'), may hold values from -0.1875 to 0.1875
- transform: bfloat16 [4096, 4096], P('wide'), may hold values from -0.125 to 0.125
- block_mask: int32 [32, 32], P('wide'), may hold values from 0 to 1, as said below
- old_index: bfloat16 [16384, 4096], P('dp', 'wide'), may hold values from -6 to 6
- doc_ids: int32 [16384, 4], P('dp'), may hold values from 0 to 16383, as said below
- labels: int32 [16384, 4], P('dp'), may hold values 0 or 1
Outputs:
- new_embed: bfloat16 [16384, 4096], P('dp', 'wide')
- pair_loss: float32 [16384, 4], P('dp')
- trunk_grad: bfloat16 [16384, 4096], P('dp', 'wide')
Inputs may be any that keep to these rules, and one draw needn't show every extreme that they name: `doc_ids`: in each aligned block of 512 rows, no shard id // 512 is named more than 128 times, and one shard is named exactly 128 times. `block_mask`: each block row has 4 to 24 nonzero entries, and some block row has exactly 24.
All inputs are finite; a program needn't handle non-finite values. No bound on the sum of `labels` on one device may be relied on, other than what follows from the above.
Results may differ from a plain program's by a relative error of at most 0.015.
Values may be sent and summed in bfloat16 or wider, within the bound.
No kernel may reach another device: no remote copies, remote signals or barrier semaphores. Data moves between devices by JAX's collectives and lax.ppermute only.
A program may use at most 128 MiB of HBM per device.

v0:
```python
import math
import jax
import jax.numpy as jnp
from jax import lax
from jax.sharding import PartitionSpec as P

E = 4096
K = 4


def local(trunk_out, projection, transform, block_mask, old_index, doc_ids, labels):
    rows = trunk_out.shape[0]
    e_local = transform.shape[0]
    width = transform.shape[1]
    local_blocks, nblocks = block_mask.shape
    side = e_local // local_blocks
    query = jnp.dot(trunk_out, projection, preferred_element_type=jnp.float32).astype(jnp.bfloat16)
    blocks = transform.reshape(local_blocks, side, nblocks, side)
    masked = (blocks * block_mask[:, None, :, None].astype(jnp.bfloat16)).reshape(e_local, width)
    term = jnp.dot(query, masked, preferred_element_type=jnp.float32)
    new = lax.psum_scatter(
        term.astype(jnp.bfloat16), "wide", scatter_dimension=1, tiled=True
    ).astype(jnp.float32)
    flat = doc_ids.reshape(-1)
    whole = lax.all_gather(old_index, "dp", axis=0, tiled=True)
    old_vec = whole[flat].reshape(rows, K, e_local)
    old_wide = old_vec.astype(jnp.float32)
    scale = 1.0 / math.sqrt(E)
    partial_scores = jnp.einsum("re,rke->rk", new, old_wide)
    score = lax.psum(partial_scores, "wide") * scale
    sign = 2.0 * labels.astype(jnp.float32) - 1.0
    pair_loss = jax.nn.softplus(-sign * score)
    dscore = -sign * jax.nn.sigmoid(-sign * score)
    grad_local = (jnp.einsum("rk,rke->re", dscore, old_wide) * scale).astype(jnp.bfloat16)
    grad_full = lax.all_gather(grad_local, "wide", axis=1, tiled=True)
    trunk_grad = lax.dot_general(
        grad_full, masked, (((1,), (1,)), ((), ())), preferred_element_type=jnp.float32
    )
    return (new.astype(jnp.bfloat16), pair_loss, trunk_grad.astype(jnp.bfloat16))


def solution(mesh):
    return jax.shard_map(
        local,
        mesh=mesh,
        in_specs=(
            P("dp", None),
            P(None, "wide"),
            P("wide", None),
            P("wide", None),
            P("dp", "wide"),
            P("dp", None),
            P("dp", None),
        ),
        out_specs=(P("dp", "wide"), P("dp", None), P("dp", "wide")),
        check_vma=False,
    )
```

profile of v0, /device:TPU:2, one launch (start us, length us, event | category | flops | bytes accessed | tf_op | source)
XLA Modules:
  0.0 241.0 jit_solution(8100249756165127333)
XLA Ops:
  8.0 0.0 copy-start
  8.0 0.0 all-gather.3.cloned.1.call-start
  8.1 0.7 all-gather.3.cloned.1.call-update
  8.7 0.0 reduce-scatter.2.cloned.1.call-start
  8.8 0.7 convert_element_type.23
  9.5 0.3 mul.36
  9.8 0.0 copy-done
  9.8 5.8 %convolution_convert_fusion = bf16[512,4096]{1,0:T(8,128)(2,1)} fusion(bf16[512,1024]{1,0:T(8,128)(2,1)S(1)} %copy-done, bf16[1024,256]{1,0:T(8,128)(2,1)} %param.8, bf16[256,4096]{1,0:T(8,128)(2,1)} %param.9, bf16[32,8,32,128]{3,2,1,0:T(8,128)(2,1)S(1)} %bitcast.21), kind=kOutput, calls=%fused_computation.1 | convolution fusion | flops 1345454080 | bytes 9961472 | tf_op jit(solution)/shard_map/dot_general | solution.py:20
  15.7 0.0 copy-start.2
  15.7 0.0 reduce-scatter.2.cloned.1.call-update
  15.7 0.0 all-gather.5.cloned.1.call-start
  15.7 0.6 copy-done.2
  16.4 0.1 copy.10
  16.5 0.2 reshape.45
  16.7 67.9 %all-gather.3.cloned.1.call-done = bf16[16384,256]{1,0:T(8,128)(2,1)} async-done(((bf16[512,256]{1,0:T(8,128)(2,1)}), bf16[16384,256]{1,0:T(8,128)(2,1)}) %all-gather.3.cloned.1.call-update) | async-done | bytes 8388624 | tf_op jit(solution)/shard_map/all_gather | solution.py:25
  84.7 13.0 %gather_fusion = bf16[2048,256]{1,0:T(8,128)(2,1)} fusion(bf16[16384,256]{1,0:T(8,128)(2,1)} %all-gather.3.cloned.1.call-done, s32[2048]{0:T(1024)S(1)} %broadcast_clamp_fusion), kind=kCustom, calls=%fused_computation | custom fusion | bytes 2105344 | tf_op jit(solution)/shard_map/gather | solution.py:26
  97.7 2.1 reshape.46
  99.8 0.0 reduce-scatter.2.cloned.1.call-done
  99.8 0.0 copy-start.1
  99.8 2.0 fusion.1
  101.8 0.1 copy.12
  101.9 31.8 %psum.7 = f32[512,4]{0,1:T(4,128)S(1)} all-reduce(f32[512,4]{0,1:T(4,128)S(1)} %bitcast.23), channel_id=1, replica_groups=mesh['dp'=32,'wide'=16] {'wide'}, use_global_device_ids=true, to_apply=%region_1.0 | all-reduce | flops 2048 | bytes 16384 | tf_op jit(solution)/shard_map/psum | solution.py:30
  133.8 0.0 copy-done.1
  133.8 0.2 copy.13
  134.0 1.9 fusion.4
  135.9 0.7 fusion
  136.7 0.0 all-gather.5.cloned.1.call-update
  136.7 0.6 compare_select_fusion.1
  137.3 91.4 %all-gather.5.cloned.1.call-done = bf16[512,4096]{1,0:T(8,128)(2,1)} async-done(((bf16[512,256]{1,0:T(8,128)(2,1)}), bf16[512,4096]{1,0:T(8,128)(2,1)}) %all-gather.5.cloned.1.call-update) | async-done | bytes 4194320 | tf_op jit(solution)/shard_map/all_gather | solution.py:35
  228.7 4.9 %convolution_convert_fusion.1 = bf16[512,256]{1,0:T(8,128)(2,1)} fusion(bf16[512,4096]{1,0:T(8,128)(2,1)} %all-gather.5.cloned.1.call-done, bf16[256,4096]{1,0:T(8,128)(2,1)} %param.9, bf16[32,8,32,128]{3,2,1,0:T(8,128)(2,1)S(1)} %bitcast.22), kind=kOutput, calls=%fused_computation.3 | convolution fusion | flops 1074921472 | bytes 8650752 | tf_op jit(solution)/shard_map/dot_general | solution.py:36
  (3 shorter events, 0.0 us)
Async XLA Ops:
  8.0 1.8 copy-start
  8.0 76.7 %all-gather.3.cloned.1.call-start = ((), (), s32[]{:S(2)}) async-start(), calls=%async_computation.2 | async-start | bytes 8650752 | tf_op jit(solution)/shard_map/all_gather | solution.py:25
  8.7 91.1 %reduce-scatter.2.cloned.1.call-start = ((), (), s32[]{:S(2)}) async-start(), calls=%async_computation.1 | async-start | bytes 4456448 | tf_op jit(solution)/shard_map/reduce_scatter | solution.py:21
  15.7 0.7 copy-start.2
  15.7 213.0 %all-gather.5.cloned.1.call-start = ((), (), s32[]{:S(2)}) async-start(), calls=%async_computation.3 | async-start | bytes 4456448 | tf_op jit(solution)/shard_map/all_gather | solution.py:35
  99.8 33.9 %copy-start.1 = (s32[512,4]{0,1:T(4,128)S(1)}, s32[512,4]{0,1:T(4,128)}, u32[]{:S(2)}) copy-start(s32[512,4]{0,1:T(4,128)} %param.13) | copy-start | bytes 24580
Sparse Core Ops, SparseCore 0:
  12.0 72.6 all-gather.2
Sparse Core Ops, SparseCore 1:
  15.8 83.9 reduce-scatter.1
  136.8 91.9 all-gather.4
where the time goes:
time: 241 us
  waiting for transfers between devices  160 us (66%)
  blocking collectives  31.8 us (13%)
  local copies, waits for them, and re-layouts  16.8 us (7%)
  between operations  15.6 us (6%)
  matrix products  14.6 us (6%)
    all_gather x1, waiting for transfers between devices, local(): grad_full = lax.all_gather(grad_local, 'wide', axis=1, tiled=True)  91.4 us
    all_gather x1, waiting for transfers between devices, local(): whole = lax.all_gather(old_index, 'dp', axis=0, tiled=True)  67.9 us
    psum x1, blocking collectives, local(): score = lax.psum(partial_scores, 'wide') * scale  31.8 us
    gather x1, local copies, waits for them, and re-layouts, local(): old_vec = whole[flat].reshape(rows, K, e_local)  13 us
    dot_general x1, matrix products, local(): term = jnp.dot(query, masked, preferred_element_type=jnp.float32)  5.83 us
    dot_general x1, matrix products, local(): lax.dot_general(grad_full, masked, (((1,), (1,)), ((), ())), preferred_el...  4.9 us
  transfers between devices with their start and end apart: 3, of which 2 were waited for; matrix products, arithmetic and copies ran while one was open for 10% of the time, Pallas kernels for 0%

commit v1 on v0

--- a/solution.py
+++ b/solution.py
@@ -32,7 +32,12 @@
     pair_loss = jax.nn.softplus(-sign * score)
     dscore = -sign * jax.nn.sigmoid(-sign * score)
     grad_local = (jnp.einsum("rk,rke->re", dscore, old_wide) * scale).astype(jnp.bfloat16)
-    grad_full = lax.all_gather(grad_local, "wide", axis=1, tiled=True)
+    grad_full = jnp.concatenate(
+        lax.all_to_all(
+            jnp.stack(lax.axis_size("wide") * [grad_local]), "wide", split_axis=0, concat_axis=0
+        ),
+        axis=1,
+    )
     trunk_grad = lax.dot_general(
         grad_full, masked, (((1,), (1,)), ((), ())), preferred_element_type=jnp.float32
     )

time: 241 us -> 341 us (1.41)
  the two profiles are of different devices: /device:TPU:2 before, /device:TPU:32 now
where the time goes in v1:
time: 341 us
  blocking collectives  220 us (65%)
  waiting for transfers between devices  68.3 us (20%)
  local copies, waits for them, and re-layouts  19.2 us (6%)
  between operations  15.6 us (5%)
  matrix products  10.4 us (3%)
  other arithmetic  7.1 us (2%)
    all_to_all x1, blocking collectives, local(): lax.all_to_all(jnp.stack(lax.axis_size('wide') * [grad_local]), 'wide', s...  190 us
    all_gather x1, waiting for transfers between devices, local(): whole = lax.all_gather(old_index, 'dp', axis=0, tiled=True)  67.6 us
    psum x1, blocking collectives, local(): score = lax.psum(partial_scores, 'wide') * scale  30.4 us
    gather x1, local copies, waits for them, and re-layouts, local(): old_vec = whole[flat].reshape(rows, K, e_local)  13 us
  transfers between devices with their start and end apart: 2, of which 1 were waited for; matrix products, arithmetic and copies ran while one was open for 7% of the time, Pallas kernels for 0%

profile of v1, /device:TPU:32, one launch (start us, length us, event | category | flops | bytes accessed | tf_op | source)
XLA Modules:
  0.0 340.9 jit_solution(11397983756455690459)
XLA Ops:
  8.0 0.0 copy-start
  8.0 0.0 all-gather.2.cloned.1.call-start
  8.1 0.7 all-gather.2.cloned.1.call-update
  8.7 0.0 reduce-scatter.2.cloned.1.call-start
  8.8 0.7 convert_element_type.23
  9.5 0.3 mul.36
  9.8 0.0 copy-done
  9.8 5.8 %convolution_convert_fusion = bf16[512,4096]{1,0:T(8,128)(2,1)} fusion(bf16[512,1024]{1,0:T(8,128)(2,1)S(1)} %copy-done, bf16[1024,256]{1,0:T(8,128)(2,1)} %param.8, bf16[256,4096]{1,0:T(8,128)(2,1)} %param.9, bf16[32,8,32,128]{3,2,1,0:T(8,128)(2,1)S(1)} %bitcast.16), kind=kOutput, calls=%fused_computation.1 | convolution fusion | flops 1345454080 | bytes 9961472 | tf_op jit(solution)/shard_map/dot_general | solution.py:20
  15.7 0.0 copy-start.2
  15.7 0.0 reduce-scatter.2.cloned.1.call-update
  15.7 0.7 copy-done.2
  16.3 0.1 copy.10
  16.5 0.2 reshape.53
  16.7 67.6 %all-gather.2.cloned.1.call-done = bf16[16384,256]{1,0:T(8,128)(2,1)} async-done(((bf16[512,256]{1,0:T(8,128)(2,1)}), bf16[16384,256]{1,0:T(8,128)(2,1)}) %all-gather.2.cloned.1.call-update) | async-done | bytes 8388624 | tf_op jit(solution)/shard_map/all_gather | solution.py:25
  84.3 13.0 %gather_fusion = bf16[2048,256]{1,0:T(8,128)(2,1)} fusion(bf16[16384,256]{1,0:T(8,128)(2,1)} %all-gather.2.cloned.1.call-done, s32[2048]{0:T(1024)S(1)} %broadcast_clamp_fusion), kind=kCustom, calls=%fused_computation | custom fusion | bytes 2105344 | tf_op jit(solution)/shard_map/gather | solution.py:26
  97.4 2.1 reshape.54
  99.5 0.0 reduce-scatter.2.cloned.1.call-done
  99.5 0.0 copy-start.3
  99.5 2.0 fusion
  101.5 0.1 copy.12
  101.6 30.4 %psum.7 = f32[512,4]{0,1:T(4,128)S(1)} all-reduce(f32[512,4]{0,1:T(4,128)S(1)} %bitcast.19), channel_id=1, replica_groups=mesh['dp'=32,'wide'=16] {'wide'}, use_global_device_ids=true, to_apply=%region_1.0 | all-reduce | flops 2048 | bytes 16384 | tf_op jit(solution)/shard_map/psum | solution.py:30
  132.0 0.0 copy-done.3
  132.0 0.6 divide_multiply_fusion
  132.7 0.1 copy.17
  132.8 4.7 %multiply_reduce_fusion = f32[512,256]{1,0:T(8,128)} fusion(bf16[512,4,256]{2,1,0:T(4,128)(2,1)} %reshape.54, f32[512,4]{1,0:T(8,128)S(1)} %copy.17), kind=kLoop, calls=%fused_computation.3 | loop fusion | flops 1441792 | bytes 1581056
  137.5 2.0 copy.16
  139.5 1.1 multiply_convert_fusion
  140.6 0.4 stack.2
  141.0 0.0 copy-start.1
  141.0 189.9 %all_to_all.5 = bf16[16,512,256]{1,2,0:T(8,128)(2,1)S(1)} all-to-all(bf16[16,512,256]{1,2,0:T(8,128)(2,1)S(1)} %stack.2), channel_id=1, replica_groups=mesh['dp'=32,'wide'=16] {'wide'}, dimensions={0} | all-to-all | bytes 8388608 | tf_op jit(solution)/shard_map/all_to_all | solution.py:36
  330.9 0.0 copy-done.1
  330.9 2.6 convolution_convert_fusion.1
  (2 shorter events, 0.0 us)
Async XLA Ops:
  8.0 1.8 copy-start
  8.0 76.3 %all-gather.2.cloned.1.call-start = ((), (), s32[]{:S(2)}) async-start(), calls=%async_computation.3 | async-start | bytes 8650752 | tf_op jit(solution)/shard_map/all_gather | solution.py:25
  8.7 90.8 %reduce-scatter.2.cloned.1.call-start = ((), (), s32[]{:S(2)}) async-start(), calls=%async_computation.2 | async-start | bytes 4456448 | tf_op jit(solution)/shard_map/reduce_scatter | solution.py:21
  15.7 0.7 copy-start.2
  99.5 32.5 %copy-start.3 = (s32[512,4]{0,1:T(4,128)S(1)}, s32[512,4]{0,1:T(4,128)}, u32[]{:S(2)}) copy-start(s32[512,4]{0,1:T(4,128)} %param.13) | copy-start | bytes 24580
  141.0 189.9 %copy-start.1 = (bf16[256,4096]{1,0:T(8,128)(2,1)S(1)}, bf16[256,4096]{1,0:T(8,128)(2,1)}, u32[]{:S(2)}) copy-start(bf16[256,4096]{1,0:T(8,128)(2,1)} %param.9) | copy-start | bytes 6291460
Sparse Core Ops, SparseCore 0:
  12.0 72.2 all-gather.1
Sparse Core Ops, SparseCore 1:
  15.8 83.3 reduce-scatter.1
